TPU v7x, 512 devices: a whole 4x8x8 slice. The times are simulated.
512 devices in a mesh: exp: 128 (over y, z, core), hid: 4 (over x).
Axes of the slice: x: 4, y: 8, z: 8, core: 2. Of those that a mesh axis runs over, the one named last changes fastest.
Arguments:
- tokens: bfloat16 [4096, 4096], P('exp', 'hid'), may hold values from -6 to 6
- expert_ids: int32 [4096, 8], P('exp'), may hold values from 0 to 127, all different within a row; in each aligned block of 16 rows (0 to 15, 16 to 31, ...) at most 2 rows name the same one
- combine: float32 [4096, 8], P('exp'), may hold values from 0.05 to 0.4
- sign_bits: int32 [128, 768], P('exp'), may hold values from 0 to 1
- w_gate: bfloat16 [128, 768, 4096], P('exp', 'hid'), may hold values from -0.09375 to 0.09375
- w_up: bfloat16 [128, 768, 4096], P('exp', 'hid'), may hold values from -0.09375 to 0.09375
- w_down: bfloat16 [128, 768, 4096], P('exp', 'hid'), may hold values from -0.21875 to 0.21875
Outputs:
- next_input: bfloat16 [4096, 4096], P('exp', 'hid')
- hessian: bfloat16 [128, 768, 768], P('exp', 'hid')
Inputs may be any that keep to these rules, and one draw needn't show every extreme that they name: `expert_ids`: each row names 8 different experts. Within each aligned block of 16 rows (one micro-batch of one index of exp) no expert is named by more than 2 rows, a bound that some block reaches. `sign_bits`: 0 stands for the sign -1, 1 for +1.
All inputs are finite; a program needn't handle non-finite values.
Results may differ from a plain program's by a relative error of at most 0.0065.
Values may be sent and summed in bfloat16 or wider, within the bound.
No kernel may reach another device: no remote copies, remote signals or barrier semaphores. Data moves between devices by JAX's collectives and lax.ppermute only.
A program may use at most 64 MiB of HBM per device.

v0:
```python
import jax
import jax.numpy as jnp
import numpy as np
from jax import lax
from jax.sharding import PartitionSpec as P


def paley_twelve():
    residues = set((number * number % 11 for number in range(1, 11)))
    legendre = [0] + [1 if number in residues else -1 for number in range(1, 11)]
    hadamard = np.zeros((12, 12))
    hadamard[0, 1:] = 1.0
    hadamard[1:, 0] = -1.0
    for row_index in range(11):
        for col_index in range(11):
            hadamard[row_index + 1, col_index + 1] = legendre[(col_index - row_index) % 11]
    return hadamard + np.eye(12)


def sylvester(order_size):
    positions = jnp.arange(order_size, dtype=jnp.int32)
    common = positions[:, None] & positions[None, :]
    parity = jnp.zeros_like(common)
    for bit_pos in range(order_size.bit_length()):
        parity = parity + (common >> bit_pos & 1)
    return (1 - 2 * (parity % 2)).astype(jnp.float32)


def rotate(hidden, sign_rows, paley_table, sylvester_table):
    values = hidden.astype(jnp.float32) * jnp.expand_dims(sign_rows, -2)
    blocks = values.reshape(values.shape[:-1] + (12, sylvester_table.shape[0]))
    turned = jnp.einsum(
        "...ab,ca,db->...cd", blocks, paley_table, sylvester_table, precision=lax.Precision.HIGHEST
    )
    return turned.reshape(values.shape)


def rank_of_pick(ids_block, experts):
    flat_ids = ids_block.reshape(-1)
    onehot = (flat_ids[:, None] == jnp.arange(experts, dtype=jnp.int32)[None, :]).astype(jnp.int32)
    before = jnp.cumsum(onehot, axis=0) - onehot
    return jnp.sum(before * onehot, axis=1).reshape(ids_block.shape)


def local(tokens, expert_ids, combine, sign_bits, w_gate, w_up, w_down):
    n_exp = lax.axis_size("exp")
    n_hid = lax.axis_size("hid")
    hid_index = lax.axis_index("hid")
    experts = w_gate.shape[0] * n_exp
    tok_rows, own_cols = tokens.shape
    half_rows = tok_rows // 2
    top_count = expert_ids.shape[1]
    capacity = min(half_rows, max(2, 2 * half_rows * top_count // experts))
    hidden_units = sign_bits.shape[1]
    share_rows = hidden_units // n_hid
    per_pair = 2 * capacity
    paley_table = jnp.asarray(paley_twelve(), jnp.float32)
    sylvester_table = sylvester(hidden_units // 12)
    sign_rows = (2 * sign_bits - 1).astype(jnp.float32)
    gram_scale = experts / (tok_rows * n_exp * top_count * hidden_units)
    down_parts = w_down[0].reshape(share_rows, n_hid, own_cols).transpose(1, 0, 2)
    down_cols = lax.all_to_all(down_parts, "hid", split_axis=0, concat_axis=0, tiled=True)
    down_cols = down_cols.reshape(hidden_units, own_cols)
    ranks = jnp.concatenate(
        [rank_of_pick(expert_ids[b * half_rows : (b + 1) * half_rows], experts) for b in range(2)],
        axis=0,
    )
    batch_of_row = (jnp.arange(tok_rows, dtype=jnp.int32) // half_rows)[:, None]
    target = expert_ids * per_pair + batch_of_row * capacity + ranks
    selector = jnp.any(
        target[None, :, :] == jnp.arange(experts * per_pair, dtype=jnp.int32)[:, None, None], axis=2
    ).astype(jnp.bfloat16)
    sending = jnp.dot(selector, tokens, preferred_element_type=jnp.float32).astype(jnp.bfloat16)
    arrived = lax.all_to_all(sending, "exp", split_axis=0, concat_axis=0, tiled=True)
    expert_in = lax.all_gather(arrived, "hid", axis=1, tiled=True)
    gate_act = jnp.dot(expert_in, w_gate[0].T, preferred_element_type=jnp.float32)
    up_act = jnp.dot(expert_in, w_up[0].T, preferred_element_type=jnp.float32)
    hidden = (jax.nn.silu(gate_act) * up_act).astype(jnp.bfloat16)
    full_hidden = lax.all_gather(hidden, "hid", axis=1, tiled=True)
    out_cols = jnp.dot(full_hidden, down_cols, preferred_element_type=jnp.float32).astype(
        jnp.bfloat16
    )
    back_rows = lax.all_to_all(out_cols, "exp", split_axis=0, concat_axis=0, tiled=True)
    picked = back_rows[target]
    mixed_rows = tokens.astype(jnp.float32) + jnp.sum(
        combine[:, :, None] * picked.astype(jnp.float32), axis=1
    )
    rotated = rotate(full_hidden, sign_rows[0], paley_table, sylvester_table)
    own_rotated = lax.dynamic_slice_in_dim(rotated, hid_index * share_rows, share_rows, 1)
    gram = jnp.dot(own_rotated.T, rotated, precision=lax.Precision.HIGHEST)
    hessian = (gram * gram_scale).astype(jnp.bfloat16)
    return (mixed_rows.astype(jnp.bfloat16), hessian[None])


def solution(mesh):
    placed = (
        P("exp", "hid"),
        P("exp", None),
        P("exp", None),
        P("exp", None),
        P("exp", "hid", None),
        P("exp", "hid", None),
        P("exp", "hid", None),
    )
    return jax.shard_map(
        local,
        mesh=mesh,
        in_specs=placed,
        out_specs=(P("exp", "hid"), P("exp", "hid", None)),
        check_vma=False,
    )
```

profile of v0, /device:TPU:1, one launch (start us, length us, event | category | flops | bytes accessed | tf_op | source)
XLA Modules:
  0.0 198.2 jit_solution(3465828189842515196)
XLA Ops:
  7.2 0.9 fusion.46
  8.4 0.2 reduce_window_sum.17
  8.5 0.2 select_reduce_fusion.1
  9.0 0.1 eq.49
  9.2 0.2 reduce_window_sum.18
  9.3 0.2 select_reduce_fusion
  9.7 0.8 compare_select_fusion
  10.5 0.2 fusion.17
  10.8 1.3 convolution_convert_fusion.1
  12.1 1.2 all_to_all.19
  13.3 48.9 %all_to_all.29 = bf16[128,4,1024]{2,1,0:T(4,128)(2,1)S(1)} all-to-all(bf16[128,4,1024]{2,1,0:T(4,128)(2,1)} %all_to_all.19), channel_id=1, replica_groups=mesh['exp'=128,'hid'=4] {'exp'}, dimensions={0} | all-to-all | bytes 2097152 | tf_op jit(solution)/shard_map/all_to_all | solution.py:74
  62.2 1.1 all_to_all.21
  63.3 2.9 %reshape_squeeze.3 = bf16[192,4,1024]{2,1,0:T(4,128)(2,1)S(1)} reshape(bf16[1,192,4096]{2,1,0:T(8,128)(2,1)} %param.14) | data formatting | bytes 3145728 | tf_op jit(solution)/shard_map/reshape;squeeze | solution.py:61
  66.2 1.7 copy.41
  67.9 4.3 %all-to-all-start.1 = ((bf16[4,192,1024]{2,1,0:T(8,128)(2,1)}), bf16[4,192,1024]{2,1,0:T(8,128)(2,1)}, u32[]{:S(2)}, u32[]{:S(2)}) async-start(bf16[4,192,1024]{2,1,0:T(8,128)(2,1)} %copy.41), calls=%async_computation.1 | async-start | bytes 3145728 | tf_op jit(solution)/shard_map/all_to_all | solution.py:62
  72.2 54.8 %all-gather.2.cloned.1.call-done = bf16[512,4096]{1,0:T(8,128)(2,1)} async-done(((bf16[512,1024]{1,0:T(8,128)(2,1)}), bf16[512,4096]{1,0:T(8,128)(2,1)}) %all-gather.2.cloned.1.call-update) | async-done | bytes 4194320 | tf_op jit(solution)/shard_map/all_gather | solution.py:75
  127.0 3.9 %fusion.4 = f32[512,192]{0,1:T(8,128)S(1)} fusion(bf16[512,4096]{1,0:T(8,128)(2,1)} %all-gather.2.cloned.1.call-done, bf16[1,192,4096]{2,1,0:T(8,128)(2,1)S(1)} %copy-done), kind=kOutput, calls=%fused_computation.5 | convolution fusion | flops 805306368 | bytes 6160384 | tf_op jit(solution)/shard_map/dot_general | solution.py:76
  130.9 1.5 fusion.12
  132.4 10.4 %all_gather.7 = bf16[512,768]{0,1:T(8,128)(2,1)S(1)} all-gather(bf16[512,192]{0,1:T(8,128)(2,1)S(1)} %fusion.12), channel_id=1, replica_groups=mesh['exp'=128,'hid'=4] {'hid'}, dimensions={1}, use_global_device_ids=true | all-gather | bytes 983040 | tf_op jit(solution)/shard_map/all_gather | solution.py:79
  142.8 2.4 %convolution_convert_fusion = bf16[512,1024]{1,0:T(8,128)(2,1)S(1)} fusion(bf16[512,768]{0,1:T(8,128)(2,1)S(1)} %all_gather.7, bf16[768,1024]{1,0:T(8,128)(2,1)} %bitcast.3), kind=kOutput, calls=%fused_computation.10 | convolution fusion | flops 805830656 | bytes 3407872 | tf_op jit(solution)/shard_map/dot_general | solution.py:80
  145.3 1.3 all_to_all.23
  146.5 11.1 %all-to-all-start.2 = ((bf16[128,4,1024]{2,1,0:T(4,128)(2,1)}), bf16[128,4,1024]{2,1,0:T(4,128)(2,1)}, u32[]{:S(2)}, u32[]{:S(2)}) async-start(bf16[128,4,1024]{2,1,0:T(4,128)(2,1)} %all_to_all.23), calls=%async_computation.2 | async-start | bytes 2097152 | tf_op jit(solution)/shard_map/all_to_all | solution.py:83
  158.0 0.2 convert_multiply_fusion
  158.2 0.2 copy-done.2
  158.4 2.6 %fusion = f32[12,512,64]{1,0,2:T(8,128)S(1)} fusion(f32[12,12,1]{1,0,2:T(8,128)S(1)} %copy-done.2, f32[512,12,64]{0,2,1:T(8,128)S(1)} %bitcast.33), kind=kOutput, calls=%fused_computation.1 | convolution fusion | flops 56623104 | bytes 3146304 | tf_op jit(solution)/shard_map/...ab,ca,db->...cd/dot_general | solution.py:32
  161.0 2.5 %fusion.6 = f32[12,512,64]{1,2,0:T(8,128)S(1)} fusion(f32[12,512,64]{1,0,2:T(8,128)S(1)} %fusion), kind=kOutput, calls=%fused_computation.7 | convolution fusion | flops 302133248 | bytes 3145728 | tf_op jit(solution)/shard_map/...ab,ca,db->...cd/dot_general | solution.py:32
  163.5 2.4 %fusion.15 = bf16[1,192,768]{2,1,0:T(8,128)(2,1)} fusion(f32[512,768]{0,1:T(8,128)S(1)} %bitcast.34, s32[]{:T(128)S(6)} %select_n.25), kind=kOutput, calls=%fused_computation.16 | convolution fusion | flops 906264576 | bytes 2260996 | tf_op jit(solution)/shard_map/dot_general | solution.py:90
  166.0 21.8 %all-to-all-done.2 = bf16[128,4,1024]{2,1,0:T(4,128)(2,1)} async-done(((bf16[128,4,1024]{2,1,0:T(4,128)(2,1)}), bf16[128,4,1024]{2,1,0:T(4,128)(2,1)}, u32[]{:S(2)}, u32[]{:S(2)}) %all-to-all-start.2) | async-done | bytes 1048608 | tf_op jit(solution)/shard_map/all_to_all | solution.py:83
  187.8 1.3 all_to_all.25
  189.1 1.2 gather_fusion
  190.3 0.4 fusion.16
  190.7 0.6 add_convert_fusion
  (32 shorter events, 1.2 us)
Async XLA Ops:
  7.2 119.8 %copy-start = (bf16[1,192,4096]{2,1,0:T(8,128)(2,1)S(1)}, bf16[1,192,4096]{2,1,0:T(8,128)(2,1)}, u32[]{:S(2)}) copy-start(bf16[1,192,4096]{2,1,0:T(8,128)(2,1)} %param.12) | copy-start | bytes 4718596
  7.2 119.8 %all-gather.2.cloned.1.call-start = ((), (), s32[]{:S(2)}) async-start(), calls=%async_computation.3 | async-start | bytes 5242880 | tf_op jit(solution)/shard_map/all_gather | solution.py:75
  67.9 75.0 %all-to-all-start.1 = ((bf16[4,192,1024]{2,1,0:T(8,128)(2,1)}), bf16[4,192,1024]{2,1,0:T(8,128)(2,1)}, u32[]{:S(2)}, u32[]{:S(2)}) async-start(bf16[4,192,1024]{2,1,0:T(8,128)(2,1)} %copy.41), calls=%async_computation.1 | async-start | bytes 3145728 | tf_op jit(solution)/shard_map/all_to_all | solution.py:62
  72.2 58.6 %copy-start.6 = (bf16[1,192,4096]{2,1,0:T(8,128)(2,1)S(1)}, bf16[1,192,4096]{2,1,0:T(8,128)(2,1)}, u32[]{:S(2)}) copy-start(bf16[1,192,4096]{2,1,0:T(8,128)(2,1)} %param.13) | copy-start | bytes 4718596
  127.0 3.9 %copy-start.5 = (bf16[512,4096]{1,0:T(8,128)(2,1)S(1)}, bf16[512,4096]{1,0:T(8,128)(2,1)}, u32[]{:S(2)}) copy-start(bf16[512,4096]{1,0:T(8,128)(2,1)} %all-gather.2.cloned.1.call-done) | copy-start | bytes 12582916
  146.5 11.3 %copy-start.3 = (f32[32,8]{0,1:T(8,128)S(1)}, f32[32,8]{0,1:T(8,128)}, u32[]{:S(2)}) copy-start(f32[32,8]{0,1:T(8,128)} %param.10) | copy-start | bytes 3076
  146.5 11.4 %copy-start.4 = (s32[1,768]{1,0:T(1,128)S(1)}, s32[1,768]{1,0:T(1,128)}, u32[]{:S(2)}) copy-start(s32[1,768]{1,0:T(1,128)} %param.11) | copy-start | bytes 9220
  146.5 41.2 %all-to-all-start.2 = ((bf16[128,4,1024]{2,1,0:T(4,128)(2,1)}), bf16[128,4,1024]{2,1,0:T(4,128)(2,1)}, u32[]{:S(2)}, u32[]{:S(2)}) async-start(bf16[128,4,1024]{2,1,0:T(4,128)(2,1)} %all_to_all.23), calls=%async_computation.2 | async-start | bytes 2097152 | tf_op jit(solution)/shard_map/all_to_all | solution.py:83
  157.7 0.7 copy-start.2
  189.1 1.6 copy-start.1
Sparse Core Ops, SparseCore 0:
  63.4 63.5 all-gather.1
where the time goes:
time: 199 us; the launch traced here: 198 us
  waiting for transfers between devices  76.6 us (38%)
  blocking collectives  59.3 us (30%)
  matrix products  16.7 us (8%)
  starting transfers between devices  15.5 us (8%)
  between operations  14.3 us (7%)
  local copies, waits for them, and re-layouts  12.7 us (6%)
  other arithmetic  3.08 us (2%)
    all_gather x1, waiting for transfers between devices, local(): expert_in = lax.all_gather(arrived, 'hid', axis=1, tiled=True)  54.8 us
    all_to_all x1, blocking collectives, local(): lax.all_to_all(sending, 'exp', split_axis=0, concat_axis=0, tiled=True)  48.9 us
    all_to_all x1, waiting for transfers between devices, local(): lax.all_to_all(out_cols, 'exp', split_axis=0, concat_axis=0, tiled=True)  21.8 us
    all_to_all x1, starting transfers between devices, local(): lax.all_to_all(out_cols, 'exp', split_axis=0, concat_axis=0, tiled=True)  11.1 us
    all_gather x1, blocking collectives, local(): full_hidden = lax.all_gather(hidden, 'hid', axis=1, tiled=True)  10.4 us
    dot_general x2, matrix products, rotate(): jnp.einsum('...ab,ca,db->...cd', blocks, paley_table, sylvester_table, pr...  5.15 us
    all_to_all x1, starting transfers between devices, local(): lax.all_to_all(down_parts, 'hid', split_axis=0, concat_axis=0, tiled=True)  4.35 us
  transfers between devices with their start and end apart: 3, of which 2 were waited for; matrix products, arithmetic and copies ran while one was open for 9% of the time, Pallas kernels for 0%

commit v1 on v0

--- a/solution.py
+++ b/solution.py
@@ -3,6 +3,13 @@
 import numpy as np
 from jax import lax
 from jax.sharding import PartitionSpec as P
+
+scales_post = lambda axis_id, arr_in: jnp.concatenate(
+    lax.all_to_all(
+        jnp.stack([arr_in for _ in range(lax.axis_size(axis_id))], axis=0), axis_id, 0, 0
+    ),
+    axis=1,
+)
 
 
 def paley_twelve():
@@ -72,7 +79,7 @@
     ).astype(jnp.bfloat16)
     sending = jnp.dot(selector, tokens, preferred_element_type=jnp.float32).astype(jnp.bfloat16)
     arrived = lax.all_to_all(sending, "exp", split_axis=0, concat_axis=0, tiled=True)
-    expert_in = lax.all_gather(arrived, "hid", axis=1, tiled=True)
+    expert_in = scales_post("hid", arrived)
     gate_act = jnp.dot(expert_in, w_gate[0].T, preferred_element_type=jnp.float32)
     up_act = jnp.dot(expert_in, w_up[0].T, preferred_element_type=jnp.float32)
     hidden = (jax.nn.silu(gate_act) * up_act).astype(jnp.bfloat16)

time: 199 us -> 195 us (0.980)
  between operations: 14.3 us -> 0.88 us
  waiting for transfers between devices: 76.6 us -> 64.4 us
  blocking collectives: 59.3 us -> 68.2 us
  starting transfers between devices: 15.5 us -> 23.6 us
  local copies, waits for them, and re-layouts: 12.7 us -> 16.6 us
    all_gather x1 -> x0, waiting for transfers between devices: 54.8 us -> none  [local(): expert_in = lax.all_gather(arrived, 'hid', axis=1, tiled=True)]
    all_to_all x0 -> x1, waiting for transfers between devices: none -> 42.6 us  [lax.all_to_all(jnp.stack([arr_in for _ in range(lax.axis_size(axis_id))],...]
    all_gather x1, blocking collectives: 10.4 us -> 19.3 us  [local(): full_hidden = lax.all_gather(hidden, 'hid', axis=1, tiled=True)]
    another operation x0 -> x3, local copies, waits for them, and re-layouts: none -> 4.91 us  [jnp.stack([arr_in for _ in range(lax.axis_size(axis_id))], axis=0)]
    all_to_all x0 -> x1, starting transfers between devices: none -> 4.86 us  [lax.all_to_all(jnp.stack([arr_in for _ in range(lax.axis_size(axis_id))],...]
    all_to_all x1, starting transfers between devices: 11.1 us -> 14.3 us  [local(): lax.all_to_all(out_cols, 'exp', split_axis=0, concat_axis=0, tiled=True)]
  transfers between devices with their start and end apart: 3 -> 3, of which waited for: 2 -> 2; matrix products, arithmetic and copies ran while one was open for 9% -> 10% of each run, Pallas kernels for 0% -> 0%
where the time goes in v1:
time: 195 us; the launch traced here: 194 us
  blocking collectives  68.2 us (35%)
  waiting for transfers between devices  64.4 us (33%)
  starting transfers between devices  23.6 us (12%)
  matrix products  17.8 us (9%)
  local copies, waits for them, and re-layouts  16.6 us (9%)
  other arithmetic  3.08 us (2%)
    all_to_all x1, blocking collectives, local(): lax.all_to_all(sending, 'exp', split_axis=0, concat_axis=0, tiled=True)  48.9 us
    all_to_all x1, waiting for transfers between devices, lax.all_to_all(jnp.stack([arr_in for _ in range(lax.axis_size(axis_id))],...  42.6 us
    all_to_all x1, waiting for transfers between devices, local(): lax.all_to_all(out_cols, 'exp', split_axis=0, concat_axis=0, tiled=True)  21.8 us
    all_gather x1, blocking collectives, local(): full_hidden = lax.all_gather(hidden, 'hid', axis=1, tiled=True)  19.3 us
    all_to_all x1, starting transfers between devices, local(): lax.all_to_all(out_cols, 'exp', split_axis=0, concat_axis=0, tiled=True)  14.3 us
    dot_general x2, matrix products, rotate(): jnp.einsum('...ab,ca,db->...cd', blocks, paley_table, sylvester_table, pr...  5.15 us
    another operation x3, local copies, waits for them, and re-layouts, jnp.stack([arr_in for _ in range(lax.axis_size(axis_id))], axis=0)  4.91 us
    all_to_all x1, starting transfers between devices, lax.all_to_all(jnp.stack([arr_in for _ in range(lax.axis_size(axis_id))],...  4.86 us
  transfers between devices with their start and end apart: 3, of which 2 were waited for; matrix products, arithmetic and copies ran while one was open for 10% of the time, Pallas kernels for 0%

profile of v1, /device:TPU:1, one launch (start us, length us, event | category | flops | bytes accessed | tf_op | source)
XLA Modules:
  0.0 194.4 jit_solution(18430582113617184645)
XLA Ops:
  0.7 0.9 fusion.46
  1.8 0.2 reduce_window_sum.17
  2.6 0.2 reduce_window_sum.18
  2.8 0.2 select_reduce_fusion
  3.1 0.8 compare_select_fusion
  4.0 0.2 fusion.17
  4.2 1.3 convolution_convert_fusion.1
  5.5 1.2 all_to_all.20
  6.7 48.9 %all_to_all.31 = bf16[128,4,1024]{2,1,0:T(4,128)(2,1)S(1)} all-to-all(bf16[128,4,1024]{2,1,0:T(4,128)(2,1)} %all_to_all.20), channel_id=1, replica_groups=mesh['exp'=128,'hid'=4] {'exp'}, dimensions={0} | all-to-all | bytes 2097152 | tf_op jit(solution)/shard_map/all_to_all | solution.py:81
  55.6 1.1 stack.4
  56.7 1.5 copy.44
  58.2 2.3 %stack.10 = bf16[4,512,1024]{1,2,0:T(8,128)(2,1)} broadcast(bf16[512,1024]{0,1:T(8,128)(2,1)S(1)} %copy.44), dimensions={1,2} | broadcast | bytes 5242880 | tf_op jit(solution)/shard_map/stack | solution.py:9
  60.5 4.9 %all-to-all-start.1 = ((bf16[4,512,1024]{1,2,0:T(8,128)(2,1)}), bf16[4,512,1024]{1,2,0:T(8,128)(2,1)}, u32[]{:S(2)}, u32[]{:S(2)}) async-start(bf16[4,512,1024]{1,2,0:T(8,128)(2,1)} %stack.10), calls=%async_computation.1 | async-start | bytes 8388608 | tf_op jit(solution)/shard_map/all_to_all | solution.py:8
  65.4 2.9 %reshape_squeeze.3 = bf16[192,4,1024]{2,1,0:T(4,128)(2,1)S(1)} reshape(bf16[1,192,4096]{2,1,0:T(8,128)(2,1)} %param.14) | data formatting | bytes 3145728 | tf_op jit(solution)/shard_map/reshape;squeeze | solution.py:68
  68.3 1.7 copy.45
  70.0 42.6 %all-to-all-done.1 = bf16[4,512,1024]{1,2,0:T(8,128)(2,1)} async-done(((bf16[4,512,1024]{1,2,0:T(8,128)(2,1)}), bf16[4,512,1024]{1,2,0:T(8,128)(2,1)}, u32[]{:S(2)}, u32[]{:S(2)}) %all-to-all-start.1) | async-done | bytes 4194336 | tf_op jit(solution)/shard_map/all_to_all | solution.py:8
  112.5 4.4 %all-to-all-start.2 = ((bf16[4,192,1024]{2,1,0:T(8,128)(2,1)}), bf16[4,192,1024]{2,1,0:T(8,128)(2,1)}, u32[]{:S(2)}, u32[]{:S(2)}) async-start(bf16[4,192,1024]{2,1,0:T(8,128)(2,1)} %copy.45), calls=%async_computation.2 | async-start | bytes 3145728 | tf_op jit(solution)/shard_map/all_to_all | solution.py:69
  116.9 3.3 %fusion.4 = f32[512,192]{0,1:T(8,128)S(1)} fusion(bf16[512,4096]{0,1:T(8,128)(2,1)} %bitcast.1, bf16[1,192,4096]{2,1,0:T(8,128)(2,1)S(1)} %copy-done), kind=kOutput, calls=%fused_computation.5 | convolution fusion | flops 805306368 | bytes 6160384 | tf_op jit(solution)/shard_map/dot_general | solution.py:83
  120.2 3.2 %fusion.12 = bf16[512,192]{0,1:T(8,128)(2,1)S(1)} fusion(bf16[512,4096]{0,1:T(8,128)(2,1)} %bitcast.1, bf16[1,192,4096]{2,1,0:T(8,128)(2,1)S(1)} %copy-done.5, f32[512,192]{0,1:T(8,128)S(1)} %fusion.4), kind=kOutput, calls=%fused_computation.15 | convolution fusion | flops 805896192 | bytes 6356992 | tf_op jit(solution)/shard_map/dot_general | solution.py:84
  123.4 19.3 %all_gather.3 = bf16[512,768]{0,1:T(8,128)(2,1)S(1)} all-gather(bf16[512,192]{0,1:T(8,128)(2,1)S(1)} %fusion.12), channel_id=1, replica_groups=mesh['exp'=128,'hid'=4] {'hid'}, dimensions={1}, use_global_device_ids=true | all-gather | bytes 983040 | tf_op jit(solution)/shard_map/all_gather | solution.py:86
  142.7 2.4 %convolution_convert_fusion = bf16[512,1024]{1,0:T(8,128)(2,1)S(1)} fusion(bf16[512,768]{0,1:T(8,128)(2,1)S(1)} %all_gather.3, bf16[768,1024]{1,0:T(8,128)(2,1)} %bitcast.6), kind=kOutput, calls=%fused_computation.10 | convolution fusion | flops 805830656 | bytes 3407872 | tf_op jit(solution)/shard_map/dot_general | solution.py:87
  145.1 1.2 all_to_all.24
  146.4 14.3 %all-to-all-start.3 = ((bf16[128,4,1024]{2,1,0:T(4,128)(2,1)}), bf16[128,4,1024]{2,1,0:T(4,128)(2,1)}, u32[]{:S(2)}, u32[]{:S(2)}) async-start(bf16[128,4,1024]{2,1,0:T(4,128)(2,1)} %all_to_all.24), calls=%async_computation.3 | async-start | bytes 2097152 | tf_op jit(solution)/shard_map/all_to_all | solution.py:90
  161.2 0.2 copy-done.2
  161.4 2.6 %fusion = f32[12,512,64]{1,0,2:T(8,128)S(1)} fusion(f32[12,12,1]{1,0,2:T(8,128)S(1)} %copy-done.2, f32[512,12,64]{0,2,1:T(8,128)S(1)} %bitcast.36), kind=kOutput, calls=%fused_computation.1 | convolution fusion | flops 56623104 | bytes 3146304 | tf_op jit(solution)/shard_map/...ab,ca,db->...cd/dot_general | solution.py:39
  164.1 2.5 %fusion.6 = f32[12,512,64]{1,2,0:T(8,128)S(1)} fusion(f32[12,512,64]{1,0,2:T(8,128)S(1)} %fusion), kind=kOutput, calls=%fused_computation.7 | convolution fusion | flops 302133248 | bytes 3145728 | tf_op jit(solution)/shard_map/...ab,ca,db->...cd/dot_general | solution.py:39
  166.6 2.4 %fusion.15 = bf16[1,192,768]{2,1,0:T(8,128)(2,1)} fusion(f32[512,768]{0,1:T(8,128)S(1)} %bitcast.37, s32[]{:T(128)S(6)} %select_n.25), kind=kOutput, calls=%fused_computation.16 | convolution fusion | flops 906264576 | bytes 2260996 | tf_op jit(solution)/shard_map/dot_general | solution.py:97
  169.0 21.8 %all-to-all-done.3 = bf16[128,4,1024]{2,1,0:T(4,128)(2,1)} async-done(((bf16[128,4,1024]{2,1,0:T(4,128)(2,1)}), bf16[128,4,1024]{2,1,0:T(4,128)(2,1)}, u32[]{:S(2)}, u32[]{:S(2)}) %all-to-all-start.3) | async-done | bytes 1048608 | tf_op jit(solution)/shard_map/all_to_all | solution.py:90
  190.8 1.3 all_to_all.26
  192.2 1.2 gather_fusion
  193.4 0.4 fusion.16
  193.8 0.6 add_convert_fusion
  (31 shorter events, 1.5 us)
Async XLA Ops:
  0.6 116.3 %copy-start = (bf16[1,192,4096]{2,1,0:T(8,128)(2,1)S(1)}, bf16[1,192,4096]{2,1,0:T(8,128)(2,1)}, u32[]{:S(2)}) copy-start(bf16[1,192,4096]{2,1,0:T(8,128)(2,1)} %param.12) | copy-start | bytes 4718596
  60.5 52.0 %all-to-all-start.1 = ((bf16[4,512,1024]{1,2,0:T(8,128)(2,1)}), bf16[4,512,1024]{1,2,0:T(8,128)(2,1)}, u32[]{:S(2)}, u32[]{:S(2)}) async-start(bf16[4,512,1024]{1,2,0:T(8,128)(2,1)} %stack.10), calls=%async_computation.1 | async-start | bytes 8388608 | tf_op jit(solution)/shard_map/all_to_all | solution.py:8
  112.5 30.2 %all-to-all-start.2 = ((bf16[4,192,1024]{2,1,0:T(8,128)(2,1)}), bf16[4,192,1024]{2,1,0:T(8,128)(2,1)}, u32[]{:S(2)}, u32[]{:S(2)}) async-start(bf16[4,192,1024]{2,1,0:T(8,128)(2,1)} %copy.45), calls=%async_computation.2 | async-start | bytes 3145728 | tf_op jit(solution)/shard_map/all_to_all | solution.py:69
  116.9 3.3 %copy-start.5 = (bf16[1,192,4096]{2,1,0:T(8,128)(2,1)S(1)}, bf16[1,192,4096]{2,1,0:T(8,128)(2,1)}, u32[]{:S(2)}) copy-start(bf16[1,192,4096]{2,1,0:T(8,128)(2,1)} %param.13) | copy-start | bytes 4718596
  146.4 14.5 %copy-start.3 = (f32[32,8]{0,1:T(8,128)S(1)}, f32[32,8]{0,1:T(8,128)}, u32[]{:S(2)}) copy-start(f32[32,8]{0,1:T(8,128)} %param.10) | copy-start | bytes 3076
  146.4 14.6 %copy-start.4 = (s32[1,768]{1,0:T(1,128)S(1)}, s32[1,768]{1,0:T(1,128)}, u32[]{:S(2)}) copy-start(s32[1,768]{1,0:T(1,128)} %param.11) | copy-start | bytes 9220
  146.4 44.4 %all-to-all-start.3 = ((bf16[128,4,1024]{2,1,0:T(4,128)(2,1)}), bf16[128,4,1024]{2,1,0:T(4,128)(2,1)}, u32[]{:S(2)}, u32[]{:S(2)}) async-start(bf16[128,4,1024]{2,1,0:T(4,128)(2,1)} %all_to_all.24), calls=%async_computation.3 | async-start | bytes 2097152 | tf_op jit(solution)/shard_map/all_to_all | solution.py:90
  160.7 0.7 copy-start.2
  192.2 1.6 copy-start.1
